TPU v7x, 256 devices: a whole 4x4x8 slice. The times are simulated.
256 devices in a mesh: row: 32 (over z, x), col: 8 (over y, core).
Axes of the slice: x: 4, y: 4, z: 8, core: 2. Of those that a mesh axis runs over, the one named last changes fastest.
Arguments:
- kernel: float32 [1, 32, 256, 4, 8, 256], P(None, 'row', None, None, 'col'), as said below
Outputs:
- factor: float32 [1, 32, 256, 4, 8, 256], P(None, 'row', None, None, 'col')
Inputs may be any that keep to these rules, and one draw needn't show every extreme that they name: kernel is a symmetric positive definite matrix.
All inputs are finite; a program needn't handle non-finite values.
Results may differ from a plain program's by a relative error of at most 0.0003.
Values sent between devices are 32-bit elements; how exact they have to be, the bound alone decides.
No kernel may reach another device: no remote copies, remote signals or barrier semaphores. Data moves between devices by JAX's collectives and lax.ppermute only.
A program may use at most 64 MiB of HBM per device.

v0:
```python
import jax
import jax.numpy as jnp
from jax import lax
from jax.scipy.linalg import solve_triangular
from jax.sharding import PartitionSpec as P

PANELS = 2
HIGHEST = lax.Precision.HIGHEST


def dot(a, b):
    return jnp.dot(a, b, precision=HIGHEST)


def col_rounds(have=PANELS):
    col_devs = lax.axis_size("col")
    rounds = []
    while have < col_devs:
        rounds.append((have, [(i, i + have) for i in range(have) if i + have < col_devs]))
        have *= 2
    return rounds


def tree_round(payload, have, pairs):
    col_id = lax.axis_index("col")
    got = lax.ppermute(payload, "col", pairs)
    return jnp.where((col_id >= have) & (col_id < 2 * have), got, payload)


def from_lead_cols(payload, have=PANELS):
    for have, pairs in col_rounds(have):
        payload = tree_round(payload, have, pairs)
    return payload


def swap_lead_cols(mine):
    col_id = lax.axis_index("col")
    other = lax.ppermute(mine, "col", [(0, 1), (1, 0)])
    return jnp.where(col_id == 0, mine, other), jnp.where(col_id == 0, other, mine)


def blocked_factor(matrix, step):
    count = matrix.shape[0] // step
    blocks = [[matrix[i * step:(i + 1) * step, j * step:(j + 1) * step] for j in range(count)] for i in range(count)]
    eye = jnp.eye(step, dtype=jnp.float32)
    low = [[None] * count for _ in range(count)]
    inv_diag = []
    for k in range(count):
        diag = jnp.linalg.cholesky(blocks[k][k])
        inv = solve_triangular(diag, eye, lower=True)
        low[k][k] = diag
        inv_diag.append(inv)
        if k + 1 < count:
            below = jnp.concatenate([blocks[i][k] for i in range(k + 1, count)], axis=0)
            below = lax.dot_general(below, inv, (((1,), (1,)), ((), ())), precision=HIGHEST)
            for i in range(k + 1, count):
                low[i][k] = below[(i - k - 1) * step:(i - k) * step]
            shrink = lax.dot_general(below, below, (((1,), (1,)), ((), ())), precision=HIGHEST)
            for i in range(k + 1, count):
                for j in range(k + 1, i + 1):
                    blocks[i][j] = blocks[i][j] - shrink[(i - k - 1) * step:(i - k) * step, (j - k - 1) * step:(j - k) * step]
    inverse = [[None] * count for _ in range(count)]
    for j in range(count):
        inverse[j][j] = inv_diag[j]
        for i in range(j + 1, count):
            acc = dot(low[i][j], inverse[j][j])
            for k in range(j + 1, i):
                acc = acc + dot(low[i][k], inverse[k][j])
            inverse[i][j] = -dot(inv_diag[i], acc)
    zero = jnp.zeros((step, step), jnp.float32)
    factor = jnp.block([[low[i][j] if j <= i else zero for j in range(count)] for i in range(count)])
    inverse = jnp.block([[inverse[i][j] if j <= i else zero for j in range(count)] for i in range(count)])
    return factor, inverse


def row_broadcast(blocks, source=0):
    row_devs = lax.axis_size("row")
    shape = blocks.shape
    send = blocks.reshape(row_devs, -1)
    piece = lax.all_to_all(send, "row", 0, 0)[source]
    send = jnp.broadcast_to(piece[None], (row_devs,) + piece.shape)
    return lax.all_to_all(send, "row", 0, 0).reshape(shape)


def shards(kernel):
    _, _, block_size, cols_local, _, _ = kernel.shape
    row_devs = lax.axis_size("row")
    row_id = lax.axis_index("row")
    col_id = lax.axis_index("col")
    lead = PANELS * block_size
    piece = block_size // row_devs
    tiles = kernel.reshape(block_size, cols_local, block_size)

    own = tiles[:, 0, :]
    swapped = lax.ppermute(own, "row", [(0, 1), (1, 0)])
    first, second = swap_lead_cols(jnp.stack([own, swapped]))
    held = from_lead_cols(jnp.concatenate([first, second]))

    send = tiles.reshape(row_devs, piece, cols_local, block_size)
    spread = lax.all_to_all(send, "row", 0, 0)[:PANELS]
    spread, held = lax.optimization_barrier((spread, held))
    row_0, row_1 = held[0], held[2]
    lead_blocks = jnp.where(row_id == 0, held[jnp.array([0, 1, 3])], held[jnp.array([1, 0, 2])])

    m00, m10, m11 = row_broadcast(lead_blocks)
    spread, m00 = lax.optimization_barrier((spread, m00))

    send = jnp.broadcast_to(spread[None], (row_devs,) + spread.shape)
    gathered = lax.all_to_all(send, "row", 0, 0)
    lead_block = gathered.transpose(1, 0, 2, 3, 4).reshape(PANELS, block_size, cols_local, block_size)

    d0, g0 = blocked_factor(m00, 128)
    l10 = lax.dot_general(m10, g0, (((1,), (1,)), ((), ())), precision=HIGHEST)
    schur = m11 - lax.dot_general(l10, l10, (((1,), (1,)), ((), ())), precision=HIGHEST)
    d1, g1 = blocked_factor(schur, 128)
    g10 = -dot(g1, dot(l10, g0))
    zero = jnp.zeros_like(d0)
    factor = jnp.block([[d0, zero], [l10, d1]])
    inverse = jnp.block([[g0, zero], [g10, g1]])

    right = dot(inverse, lead_block.reshape(lead, cols_local * block_size))
    left = lax.dot_general(
        jnp.concatenate([row_0, row_1], axis=1), inverse, (((1,), (1,)), ((), ())), precision=HIGHEST
    )
    left = jnp.where(
        row_id == 0,
        factor[:block_size],
        jnp.where(row_id == 1, factor[block_size:], left),
    )
    update = dot(left, right).reshape(block_size, cols_local, block_size)
    trailing = jnp.where(row_id >= PANELS, tiles - update, 0.0)
    panel = jnp.where(col_id == 0, left[:, :block_size], left[:, block_size:])
    first_col = jnp.where(col_id < PANELS, panel, trailing[:, 0, :])
    out = trailing.at[:, 0, :].set(first_col)
    return out.reshape(kernel.shape)


def solution(mesh):
    in_specs = (P(None, "row", None, None, "col", None),)
    out_specs = P(None, "row", None, None, "col", None)
    return jax.shard_map(shards, mesh=mesh, in_specs=in_specs, out_specs=out_specs, check_vma=False)
```

profile of v0, /device:TPU:26, one launch (start us, length us, event | category | flops | bytes accessed | tf_op | source)
XLA Modules:
  0.0 256.0 jit_solution(11261126747227191817)
XLA Ops:
  0.0 1.4 copy.81
  1.5 2.4 collective-permute-start
  3.9 7.5 %collective-permute-done = f32[256,256]{1,0:T(8,128)S(1)} collective-permute-done((f32[256,256]{1,0:T(8,128)S(1)}, f32[256,256]{1,0:T(8,128)S(1)}, u32[]{:S(2)}, u32[]{:S(2)}) %collective-permute-start) | collective-permute-done | bytes 262176 | tf_op jit(solution)/shard_map/ppermute | solution.py:95
  12.4 1.8 collective-permute-start.2
  15.5 4.8 %all-to-all-start = ((f32[32,8,4,256]{3,2,1,0:T(4,128)}), f32[32,8,4,256]{3,2,1,0:T(4,128)}, u32[]{:S(2)}, u32[]{:S(2)}) async-start(f32[32,8,4,256]{3,2,1,0:T(4,128)} %bitcast.26), calls=%async_computation | async-start | bytes 2097152 | tf_op jit(solution)/shard_map/all_to_all | solution.py:100
  20.4 1.3 collective-permute-start.3
  21.8 26.1 %all-to-all-done = f32[32,8,4,256]{3,2,1,0:T(4,128)} async-done(((f32[32,8,4,256]{3,2,1,0:T(4,128)}), f32[32,8,4,256]{3,2,1,0:T(4,128)}, u32[]{:S(2)}, u32[]{:S(2)}) %all-to-all-start) | async-done | bytes 1048608 | tf_op jit(solution)/shard_map/all_to_all | solution.py:100
  48.7 18.9 %collective-permute-done.3 = f32[4,256,256]{2,1,0:T(8,128)} collective-permute-done((f32[4,256,256]{2,1,0:T(8,128)S(1)}, f32[4,256,256]{2,1,0:T(8,128)}, u32[]{:S(2)}, u32[]{:S(2)}) %collective-permute-start.3) | collective-permute-done | bytes 1048608 | tf_op jit(solution)/shard_map/ppermute | solution.py:26
  67.6 1.4 broadcast_select_fusion.2
  69.6 1.5 gather_fusion
  72.0 1.9 select_n.126
  74.0 26.3 %all_to_all.22 = f32[32,1,6144]{2,1,0:T(1,128)S(1)} all-to-all(f32[32,1,6144]{2,1,0:T(1,128)S(1)} %select_n.126), channel_id=1, replica_groups=mesh['row'=32,'col'=8] {'row'}, dimensions={0} | all-to-all | bytes 1572864 | tf_op jit(solution)/shard_map/all_to_all | solution.py:80
  100.3 1.3 broadcast_in_dim.27
  101.6 5.8 %all-to-all-start.2 = ((f32[32,1,6144]{2,1,0:T(1,128)}), f32[32,1,6144]{2,1,0:T(1,128)S(1)}, u32[]{:S(2)}, u32[]{:S(2)}) async-start(f32[32,1,6144]{2,1,0:T(1,128)} %broadcast_in_dim.27), calls=%async_computation.2 | async-start | bytes 1572864 | tf_op jit(solution)/shard_map/all_to_all | solution.py:82
  108.2 20.3 %all-to-all-done.2 = f32[32,1,6144]{2,1,0:T(1,128)S(1)} async-done(((f32[32,1,6144]{2,1,0:T(1,128)}), f32[32,1,6144]{2,1,0:T(1,128)S(1)}, u32[]{:S(2)}, u32[]{:S(2)}) %all-to-all-start.2) | async-done | bytes 786464 | tf_op jit(solution)/shard_map/all_to_all | solution.py:82
  128.4 1.9 reduce.6
  130.7 11.7 %cholesky.74 = f32[128,128]{1,0:T(8,128)S(1)} custom-call(f32[128,128]{1,0:T(8,128)S(1)} %fusion.34), custom_call_target="Cholesky" | custom-call | tf_op jit(solution)/shard_map/jit(cholesky)/cholesky | solution.py:49
  143.8 9.8 %custom-call.8 = f32[1,128,128]{1,2,0:T(8,128)S(1)} custom-call(f32[1,128,128]{2,1,0:T(8,128)S(1)} %get-tuple-element.33), custom_call_target="InvertDiagBlocksLowerTriangular" | custom-call | tf_op jit(solution)/shard_map/jit(_solve_triangular)/triangular_solve | solution.py:50
  154.8 12.1 %cholesky.85 = f32[128,128]{1,0:T(8,128)S(1)} custom-call(f32[128,128]{1,0:T(8,128)S(1)} %fusion.32), custom_call_target="Cholesky" | custom-call | tf_op jit(solution)/shard_map/jit(cholesky)/cholesky | solution.py:49
  168.3 9.8 %custom-call.9 = f32[1,128,128]{1,2,0:T(8,128)S(1)} custom-call(f32[1,128,128]{2,1,0:T(8,128)S(1)} %get-tuple-element.31), custom_call_target="InvertDiagBlocksLowerTriangular" | custom-call | tf_op jit(solution)/shard_map/jit(_solve_triangular)/triangular_solve | solution.py:50
  178.4 1.8 broadcast_in_dim.28
  180.2 5.6 %all-to-all-start.3 = ((f32[32,2,8,4,256]{4,3,2,1,0:T(4,128)}), f32[32,2,8,4,256]{4,3,2,1,0:T(4,128)}, u32[]{:S(2)}, u32[]{:S(2)}) async-start(f32[32,2,8,4,256]{4,3,2,1,0:T(4,128)} %broadcast_in_dim.28), calls=%async_computation.3 | async-start | bytes 4194304 | tf_op jit(solution)/shard_map/all_to_all | solution.py:109
  188.4 11.7 %cholesky.96 = f32[128,128]{1,0:T(8,128)S(1)} custom-call(f32[128,128]{1,0:T(8,128)S(1)} %fusion.30), custom_call_target="Cholesky" | custom-call | tf_op jit(solution)/shard_map/jit(cholesky)/cholesky | solution.py:49
  201.6 9.8 %custom-call.10 = f32[1,128,128]{1,2,0:T(8,128)S(1)} custom-call(f32[1,128,128]{2,1,0:T(8,128)S(1)} %get-tuple-element.29), custom_call_target="InvertDiagBlocksLowerTriangular" | custom-call | tf_op jit(solution)/shard_map/jit(_solve_triangular)/triangular_solve | solution.py:50
  212.4 11.7 %cholesky.107 = f32[128,128]{1,0:T(8,128)S(1)} custom-call(f32[128,128]{1,0:T(8,128)S(1)} %fusion.28), custom_call_target="Cholesky" | custom-call | tf_op jit(solution)/shard_map/jit(cholesky)/cholesky | solution.py:49
  225.6 9.9 %custom-call.11 = f32[1,128,128]{1,2,0:T(8,128)S(1)} custom-call(f32[1,128,128]{2,1,0:T(8,128)S(1)} %get-tuple-element.27), custom_call_target="InvertDiagBlocksLowerTriangular" | custom-call | tf_op jit(solution)/shard_map/jit(_solve_triangular)/triangular_solve | solution.py:50
  237.6 2.1 fusion
  239.7 2.1 copy.63
  242.3 3.5 %fusion.6 = f32[512,1024]{1,0:T(8,128)S(1)} fusion(f32[512,1024]{1,0:T(8,128)S(1)} %bitcast.86, f32[256,256]{1,0:T(8,128)S(1)} %get-tuple-element.43, f32[128,128]{1,0:T(8,128)S(1)} %copy.61, f32[128,128]{1,0:T(8,128)S(1)} %convolution_negate_fusion.1, f32[128,256]{1,0:T(8,128)S(1)} %concatenate.80, f32[256,256]{1,0:T(8,128)S(1)} %convolution_negate_fusion), kind=kOutput, calls=%fused_computation.26 | convolution fusion | flops 3222798336 | bytes 4980736 | tf_op jit(solution)/shard_map/dot_general | solution.py:12
  245.9 1.9 fusion.48
  247.8 1.3 copy.65
  251.5 2.3 broadcast_select_fusion
  (86 shorter events, 23.4 us)
Async XLA Ops:
  1.4 10.7 %copy-start.1 = (f32[1,1,256,4,1,256]{5,2,3,4,1,0:T(8,128)}, f32[1,1,256,4,1,256]{5,2,3,4,1,0:T(8,128)S(1)}, u32[]{:S(2)}) copy-start(f32[1,1,256,4,1,256]{5,2,3,4,1,0:T(8,128)S(1)} %copy.81) | copy-start | bytes 3145732
  1.5 9.9 %collective-permute-start = (f32[256,256]{1,0:T(8,128)S(1)}, f32[256,256]{1,0:T(8,128)S(1)}, u32[]{:S(2)}, u32[]{:S(2)}) collective-permute-start(f32[256,256]{1,0:T(8,128)S(1)} %get-tuple-element.40), channel_id=1, source_target_pairs={{0,8},{8,0},{1,9},{9,1},{2,10},{10,2},{3,11},{11,3},{4,12},{12,4},... | collective-permute-start | bytes 786440 | tf_op jit(solution)/shard_map/ppermute | solution.py:95
  11.5 0.7 collective-permute-start.1
  12.2 2.0 copy-start
  12.4 7.9 %collective-permute-start.2 = (f32[4,256,256]{2,1,0:T(8,128)S(1)}, f32[4,256,256]{2,1,0:T(8,128)}, u32[]{:S(2)}, u32[]{:S(2)}) collective-permute-start(f32[4,256,256]{2,1,0:T(8,128)S(1)} %pad_maximum_fusion), channel_id=1, source_target_pairs={{0,2},{1,3},{8,10},{9,11},{16,18},{17,19},{24,26},{25,27},{32,34},... | collective-permute-start | bytes 3145736 | tf_op jit(solution)/shard_map/ppermute | solution.py:26
  15.5 32.4 %all-to-all-start = ((f32[32,8,4,256]{3,2,1,0:T(4,128)}), f32[32,8,4,256]{3,2,1,0:T(4,128)}, u32[]{:S(2)}, u32[]{:S(2)}) async-start(f32[32,8,4,256]{3,2,1,0:T(4,128)} %bitcast.26), calls=%async_computation | async-start | bytes 2097152 | tf_op jit(solution)/shard_map/all_to_all | solution.py:100
  20.2 1.5 copy-start.6
  20.3 1.5 copy-start.5
  20.4 47.2 %collective-permute-start.3 = (f32[4,256,256]{2,1,0:T(8,128)S(1)}, f32[4,256,256]{2,1,0:T(8,128)}, u32[]{:S(2)}, u32[]{:S(2)}) collective-permute-start(f32[4,256,256]{2,1,0:T(8,128)S(1)} %broadcast_select_fusion.1), channel_id=1, source_target_pairs={{0,4},{1,5},{2,6},{3,7},{8,12},{9,13},{10,14},{11,15},{16,20},{17,... | collective-permute-start | bytes 3145736 | tf_op jit(solution)/shard_map/ppermute | solution.py:26
  101.6 26.9 %all-to-all-start.2 = ((f32[32,1,6144]{2,1,0:T(1,128)}), f32[32,1,6144]{2,1,0:T(1,128)S(1)}, u32[]{:S(2)}, u32[]{:S(2)}) async-start(f32[32,1,6144]{2,1,0:T(1,128)} %broadcast_in_dim.27), calls=%async_computation.2 | async-start | bytes 1572864 | tf_op jit(solution)/shard_map/all_to_all | solution.py:82
  180.2 59.5 %all-to-all-start.3 = ((f32[32,2,8,4,256]{4,3,2,1,0:T(4,128)}), f32[32,2,8,4,256]{4,3,2,1,0:T(4,128)}, u32[]{:S(2)}, u32[]{:S(2)}) async-start(f32[32,2,8,4,256]{4,3,2,1,0:T(4,128)} %broadcast_in_dim.28), calls=%async_computation.3 | async-start | bytes 4194304 | tf_op jit(solution)/shard_map/all_to_all | solution.py:109
  212.0 25.6 %copy-start.4 = (f32[256,256]{1,0:T(8,128)S(1)}, f32[256,256]{1,0:T(8,128)}, u32[]{:S(2)}) copy-start(f32[256,256]{1,0:T(8,128)} %copy.59) | copy-start | bytes 786436
  239.6 6.2 %copy-start.2 = (f32[256,512]{1,0:T(8,128)}, f32[256,512]{1,0:T(8,128)S(1)}, u32[]{:S(2)}) copy-start(f32[256,512]{1,0:T(8,128)S(1)} %fusion) | copy-start | bytes 1572868
  250.3 3.5 %copy-start.3 = (f32[256,512]{1,0:T(8,128)S(1)}, f32[256,512]{1,0:T(8,128)}, u32[]{:S(2)}) copy-start(f32[256,512]{1,0:T(8,128)} %copy-done.2) | copy-start | bytes 1572868
where the time goes:
time: 260 us; the launch traced here: 256 us
  other arithmetic  100 us (38%)
  waiting for transfers between devices  72.7 us (28%)
  blocking collectives  26.3 us (10%)
  starting transfers between devices  22.4 us (9%)
  local copies, waits for them, and re-layouts  20.8 us (8%)
  matrix products  12.7 us (5%)
    another operation x12, other arithmetic, blocked_factor(): diag = jnp.linalg.cholesky(blocks[k][k])  50.1 us
    another operation x8, other arithmetic, blocked_factor(): inv = solve_triangular(diag, eye, lower=True)  42.1 us
    all_to_all x1, blocking collectives, row_broadcast(): piece = lax.all_to_all(send, 'row', 0, 0)[source]  26.3 us
    all_to_all x1, waiting for transfers between devices, shards(): spread = lax.all_to_all(send, 'row', 0, 0)[:PANELS]  26.1 us
    all_to_all x1, waiting for transfers between devices, row_broadcast(): return lax.all_to_all(send, 'row', 0, 0).reshape(shape)  20.3 us
    ppermute x2, waiting for transfers between devices, tree_round(): got = lax.ppermute(payload, 'col', pairs)  18.9 us
    dot_general x8, matrix products, dot(): return jnp.dot(a, b, precision=HIGHEST)  7.56 us
    ppermute x1, waiting for transfers between devices, shards(): swapped = lax.ppermute(own, 'row', [(0, 1), (1, 0)])  7.49 us
  transfers between devices with their start and end apart: 7, of which 4 were waited for; matrix products, arithmetic and copies ran while one was open for 22% of the time, Pallas kernels for 0%

commit v1 on v0

--- a/solution.py
+++ b/solution.py
@@ -82,6 +82,15 @@
     return lax.all_to_all(send, "row", 0, 0).reshape(shape)
 
 
+def lead_rows_from(blocks):
+    row_devs = lax.axis_size("row")
+    send = blocks.reshape(row_devs, -1)
+    piece = lax.all_to_all(send, "row", 0, 0)[:PANELS]
+    send = jnp.broadcast_to(piece[None], (row_devs,) + piece.shape)
+    gathered = lax.all_to_all(send, "row", 0, 0)
+    return gathered.swapaxes(0, 1).reshape((PANELS,) + blocks.shape)
+
+
 def shards(kernel):
     _, _, block_size, cols_local, _, _ = kernel.shape
     row_devs = lax.axis_size("row")
@@ -91,18 +100,16 @@
     piece = block_size // row_devs
     tiles = kernel.reshape(block_size, cols_local, block_size)
 
-    own = tiles[:, 0, :]
-    swapped = lax.ppermute(own, "row", [(0, 1), (1, 0)])
-    first, second = swap_lead_cols(jnp.stack([own, swapped]))
-    held = from_lead_cols(jnp.concatenate([first, second]))
+    first, second = swap_lead_cols(tiles[:, 0, :])
+    held = from_lead_cols(jnp.stack([first, second]))
 
     send = tiles.reshape(row_devs, piece, cols_local, block_size)
     spread = lax.all_to_all(send, "row", 0, 0)[:PANELS]
     spread, held = lax.optimization_barrier((spread, held))
-    row_0, row_1 = held[0], held[2]
-    lead_blocks = jnp.where(row_id == 0, held[jnp.array([0, 1, 3])], held[jnp.array([1, 0, 2])])
+    row_0, row_1 = held[0], held[1]
 
-    m00, m10, m11 = row_broadcast(lead_blocks)
+    lead_rows = lead_rows_from(held)
+    m00, m10, m11 = lead_rows[0, 0], lead_rows[1, 0], lead_rows[1, 1]
     spread, m00 = lax.optimization_barrier((spread, m00))
 
     send = jnp.broadcast_to(spread[None], (row_devs,) + spread.shape)

time: 260 us -> 235 us (0.904)
  waiting for transfers between devices: 72.7 us -> 50.9 us
  starting transfers between devices: 22.4 us -> 25.7 us
  other arithmetic: 100 us -> 96.7 us
    all_to_all x1, waiting for transfers between devices: 26.1 us -> 0.01 us  [shards(): spread = lax.all_to_all(send, 'row', 0, 0)[:PANELS]]
    ppermute x1 -> x0, waiting for transfers between devices: 7.49 us -> none  [shards(): swapped = lax.ppermute(own, 'row', [(0, 1), (1, 0)])]
    ppermute x2, waiting for transfers between devices: 18.9 us -> 26.1 us  [tree_round(): got = lax.ppermute(payload, 'col', pairs)]
    all_to_all x1, starting transfers between devices: 4.77 us -> 11.7 us  [shards(): spread = lax.all_to_all(send, 'row', 0, 0)[:PANELS]]
    all_to_all x1, waiting for transfers between devices: 20.3 us -> 24.9 us  [lead_rows_from(): gathered = lax.all_to_all(send, 'row', 0, 0)]
  transfers between devices with their start and end apart: 7 -> 6, of which waited for: 4 -> 2; matrix products, arithmetic and copies ran while one was open for 22% -> 24% of each run, Pallas kernels for 0% -> 0%
where the time goes in v1:
time: 235 us; the launch traced here: 232 us
  other arithmetic  96.7 us (41%)
  waiting for transfers between devices  50.9 us (22%)
  starting transfers between devices  25.7 us (11%)
  blocking collectives  24.5 us (10%)
  local copies, waits for them, and re-layouts  20.4 us (9%)
  matrix products  12.6 us (5%)
    another operation x12, other arithmetic, blocked_factor(): diag = jnp.linalg.cholesky(blocks[k][k])  49.6 us
    another operation x8, other arithmetic, blocked_factor(): inv = solve_triangular(diag, eye, lower=True)  43.5 us
    ppermute x2, waiting for transfers between devices, tree_round(): got = lax.ppermute(payload, 'col', pairs)  26.1 us
    all_to_all x1, waiting for transfers between devices, lead_rows_from(): gathered = lax.all_to_all(send, 'row', 0, 0)  24.9 us
    all_to_all x1, blocking collectives, lead_rows_from(): piece = lax.all_to_all(send, 'row', 0, 0)[:PANELS]  24.5 us
    all_to_all x1, starting transfers between devices, shards(): spread = lax.all_to_all(send, 'row', 0, 0)[:PANELS]  11.7 us
    dot_general x8, matrix products, dot(): return jnp.dot(a, b, precision=HIGHEST)  7.55 us
    all_to_all x1, starting transfers between devices, lead_rows_from(): gathered = lax.all_to_all(send, 'row', 0, 0)  5.74 us
  transfers between devices with their start and end apart: 6, of which 2 were waited for; matrix products, arithmetic and copies ran while one was open for 24% of the time, Pallas kernels for 0%

profile of v1, /device:TPU:26, one launch (start us, length us, event | category | flops | bytes accessed | tf_op | source)
XLA Modules:
  0.0 231.7 jit_solution(7686136871257038691)
XLA Ops:
  0.0 1.5 copy.82
  2.3 1.2 copy.73
  3.5 11.7 %all-to-all-start = ((f32[32,8,4,256]{3,2,1,0:T(4,128)}), f32[32,8,4,256]{3,2,1,0:T(4,128)}, u32[]{:S(2)}, u32[]{:S(2)}) async-start(f32[32,8,4,256]{3,2,1,0:T(4,128)} %bitcast.26), calls=%async_computation | async-start | bytes 2097152 | tf_op jit(solution)/shard_map/all_to_all | solution.py:107
  16.1 1.3 collective-permute-start.2
  17.4 26.1 %collective-permute-done.2 = f32[2,256,256]{2,1,0:T(8,128)S(1)} collective-permute-done((f32[2,256,256]{2,1,0:T(8,128)S(1)}, f32[2,256,256]{2,1,0:T(8,128)S(1)}, u32[]{:S(2)}, u32[]{:S(2)}) %collective-permute-start.2) | collective-permute-done | bytes 524320 | tf_op jit(solution)/shard_map/ppermute | solution.py:26
  45.0 24.5 %all_to_all.25 = f32[32,1,4096]{2,1,0:T(1,128)S(1)} all-to-all(f32[32,1,4096]{2,1,0:T(1,128)S(1)} %all_to_all.20), channel_id=1, replica_groups=mesh['row'=32,'col'=8] {'row'}, dimensions={0} | all-to-all | bytes 1048576 | tf_op jit(solution)/shard_map/all_to_all | solution.py:88
  69.5 1.4 broadcast_in_dim.23
  71.0 5.7 %all-to-all-start.2 = ((f32[32,2,4096]{2,1,0:T(2,128)}), f32[32,2,4096]{2,1,0:T(2,128)S(1)}, u32[]{:S(2)}, u32[]{:S(2)}) async-start(f32[32,2,4096]{2,1,0:T(2,128)} %broadcast_in_dim.23), calls=%async_computation.2 | async-start | bytes 2097152 | tf_op jit(solution)/shard_map/all_to_all | solution.py:90
  77.6 24.9 %all-to-all-done.2 = f32[32,2,4096]{2,1,0:T(2,128)S(1)} async-done(((f32[32,2,4096]{2,1,0:T(2,128)}), f32[32,2,4096]{2,1,0:T(2,128)S(1)}, u32[]{:S(2)}, u32[]{:S(2)}) %all-to-all-start.2) | async-done | bytes 1048608 | tf_op jit(solution)/shard_map/all_to_all | solution.py:90
  102.4 1.6 copy.44
  104.0 1.4 reshape.66
  105.7 11.7 %cholesky.74 = f32[128,128]{1,0:T(8,128)S(1)} custom-call(f32[128,128]{1,0:T(8,128)S(1)} %fusion.34), custom_call_target="Cholesky" | custom-call | tf_op jit(solution)/shard_map/jit(cholesky)/cholesky | solution.py:49
  118.8 9.8 %custom-call.8 = f32[1,128,128]{1,2,0:T(8,128)S(1)} custom-call(f32[1,128,128]{2,1,0:T(8,128)S(1)} %get-tuple-element.33), custom_call_target="InvertDiagBlocksLowerTriangular" | custom-call | tf_op jit(solution)/shard_map/jit(_solve_triangular)/triangular_solve | solution.py:50
  129.8 11.7 %cholesky.85 = f32[128,128]{1,0:T(8,128)S(1)} custom-call(f32[128,128]{1,0:T(8,128)S(1)} %fusion.32), custom_call_target="Cholesky" | custom-call | tf_op jit(solution)/shard_map/jit(cholesky)/cholesky | solution.py:49
  142.8 10.2 %custom-call.9 = f32[1,128,128]{1,2,0:T(8,128)S(1)} custom-call(f32[1,128,128]{2,1,0:T(8,128)S(1)} %get-tuple-element.31), custom_call_target="InvertDiagBlocksLowerTriangular" | custom-call | tf_op jit(solution)/shard_map/jit(_solve_triangular)/triangular_solve | solution.py:50
  153.3 1.8 broadcast_in_dim.24
  155.1 5.6 %all-to-all-start.3 = ((f32[32,2,8,4,256]{4,3,2,1,0:T(4,128)}), f32[32,2,8,4,256]{4,3,2,1,0:T(4,128)}, u32[]{:S(2)}, u32[]{:S(2)}) async-start(f32[32,2,8,4,256]{4,3,2,1,0:T(4,128)} %broadcast_in_dim.24), calls=%async_computation.3 | async-start | bytes 4194304 | tf_op jit(solution)/shard_map/all_to_all | solution.py:116
  162.7 11.7 %cholesky.96 = f32[128,128]{1,0:T(8,128)S(1)} custom-call(f32[128,128]{1,0:T(8,128)S(1)} %fusion.30), custom_call_target="Cholesky" | custom-call | tf_op jit(solution)/shard_map/jit(cholesky)/cholesky | solution.py:49
  175.0 1.2 select_bitcast_fusion.3
  176.2 9.8 %custom-call.10 = f32[1,128,128]{1,2,0:T(8,128)S(1)} custom-call(f32[1,128,128]{2,1,0:T(8,128)S(1)} %get-tuple-element.29), custom_call_target="InvertDiagBlocksLowerTriangular" | custom-call | tf_op jit(solution)/shard_map/jit(_solve_triangular)/triangular_solve | solution.py:50
  187.7 11.7 %cholesky.107 = f32[128,128]{1,0:T(8,128)S(1)} custom-call(f32[128,128]{1,0:T(8,128)S(1)} %fusion.28), custom_call_target="Cholesky" | custom-call | tf_op jit(solution)/shard_map/jit(cholesky)/cholesky | solution.py:49
  200.1 1.2 select_bitcast_fusion.2
  201.3 10.0 %custom-call.11 = f32[1,128,128]{1,2,0:T(8,128)S(1)} custom-call(f32[1,128,128]{2,1,0:T(8,128)S(1)} %get-tuple-element.27), custom_call_target="InvertDiagBlocksLowerTriangular" | custom-call | tf_op jit(solution)/shard_map/jit(_solve_triangular)/triangular_solve | solution.py:50
  213.3 2.0 fusion
  215.4 2.1 copy.62
  218.0 3.5 %fusion.6 = f32[512,1024]{1,0:T(8,128)S(1)} fusion(f32[512,1024]{1,0:T(8,128)S(1)} %bitcast.94, f32[256,256]{1,0:T(8,128)S(1)} %get-tuple-element.41, f32[128,128]{1,0:T(8,128)S(1)} %copy.60, f32[128,128]{1,0:T(8,128)S(1)} %convolution_negate_fusion.1, f32[128,256]{1,0:T(8,128)S(1)} %concatenate.76, f32[256,256]{1,0:T(8,128)S(1)} %convolution_negate_fusion), kind=kOutput, calls=%fused_computation.21 | convolution fusion | flops 3222798336 | bytes 4980736 | tf_op jit(solution)/shard_map/dot_general | solution.py:12
  221.6 1.9 fusion.48
  223.5 1.3 copy.64
  224.8 1.2 reshape.70
  226.0 1.0 slice.111
  227.2 2.3 %broadcast_select_fusion = f32[1,1,256,4,1,256]{5,4,3,2,1,0:T(1,128)} fusion(pred[]{:T(512)S(6)} %ge.12, f32[1,1,256,4,1,256]{5,4,3,2,1,0:T(1,128)S(1)} %copy-done, f32[1,1,256,4,1,256]{5,4,3,2,1,0:T(1,128)S(1)} %reshape.70), kind=kLoop, calls=%fused_computation | loop fusion | flops 524288 | bytes 3145729 | tf_op jit(solution)/shard_map/jit(_where)/select_n | solution.py:138
  229.5 1.0 fusion.8
  (79 shorter events, 16.6 us)
Async XLA Ops:
  0.0 2.2 copy-start
  1.5 13.7 %copy-start.1 = (f32[1,1,256,4,1,256]{5,2,3,4,1,0:T(8,128)}, f32[1,1,256,4,1,256]{5,2,3,4,1,0:T(8,128)S(1)}, u32[]{:S(2)}) copy-start(f32[1,1,256,4,1,256]{5,2,3,4,1,0:T(8,128)S(1)} %copy.82) | copy-start | bytes 3145732
  1.6 13.6 %collective-permute-start = (f32[256,256]{1,0:T(8,128)S(1)}, f32[256,256]{1,0:T(8,128)S(1)}, u32[]{:S(2)}, u32[]{:S(2)}) collective-permute-start(f32[256,256]{1,0:T(8,128)S(1)} %slice_bitcast_fusion.4), channel_id=1, source_target_pairs={{0,1},{1,0},{8,9},{9,8},{16,17},{17,16},{24,25},{25,24},{32,33},{3... | collective-permute-start | bytes 786440 | tf_op jit(solution)/shard_map/ppermute | solution.py:38
  3.5 40.1 %all-to-all-start = ((f32[32,8,4,256]{3,2,1,0:T(4,128)}), f32[32,8,4,256]{3,2,1,0:T(4,128)}, u32[]{:S(2)}, u32[]{:S(2)}) async-start(f32[32,8,4,256]{3,2,1,0:T(4,128)} %bitcast.26), calls=%async_computation | async-start | bytes 2097152 | tf_op jit(solution)/shard_map/all_to_all | solution.py:107
  15.3 0.7 collective-permute-start.1
  16.1 27.4 %collective-permute-start.2 = (f32[2,256,256]{2,1,0:T(8,128)S(1)}, f32[2,256,256]{2,1,0:T(8,128)S(1)}, u32[]{:S(2)}, u32[]{:S(2)}) collective-permute-start(f32[2,256,256]{2,1,0:T(8,128)S(1)} %broadcast_select_fusion.1), channel_id=1, source_target_pairs={{0,4},{1,5},{2,6},{3,7},{8,12},{9,13},{10,14},{11,15},{16,20},{17,... | collective-permute-start | bytes 1572872 | tf_op jit(solution)/shard_map/ppermute | solution.py:26
  71.0 31.5 %all-to-all-start.2 = ((f32[32,2,4096]{2,1,0:T(2,128)}), f32[32,2,4096]{2,1,0:T(2,128)S(1)}, u32[]{:S(2)}, u32[]{:S(2)}) async-start(f32[32,2,4096]{2,1,0:T(2,128)} %broadcast_in_dim.23), calls=%async_computation.2 | async-start | bytes 2097152 | tf_op jit(solution)/shard_map/all_to_all | solution.py:90
  155.1 60.3 %all-to-all-start.3 = ((f32[32,2,8,4,256]{4,3,2,1,0:T(4,128)}), f32[32,2,8,4,256]{4,3,2,1,0:T(4,128)}, u32[]{:S(2)}, u32[]{:S(2)}) async-start(f32[32,2,8,4,256]{4,3,2,1,0:T(4,128)} %broadcast_in_dim.24), calls=%async_computation.3 | async-start | bytes 4194304 | tf_op jit(solution)/shard_map/all_to_all | solution.py:116
  187.3 26.0 %copy-start.4 = (f32[256,256]{1,0:T(8,128)S(1)}, f32[256,256]{1,0:T(8,128)}, u32[]{:S(2)}) copy-start(f32[256,256]{1,0:T(8,128)} %get-tuple-element.39) | copy-start | bytes 786436
  211.7 1.7 copy-start.5
  211.7 1.7 copy-start.6
  215.4 6.2 %copy-start.2 = (f32[256,512]{1,0:T(8,128)}, f32[256,512]{1,0:T(8,128)S(1)}, u32[]{:S(2)}) copy-start(f32[256,512]{1,0:T(8,128)S(1)} %fusion) | copy-start | bytes 1572868
  226.0 3.5 %copy-start.3 = (f32[256,512]{1,0:T(8,128)S(1)}, f32[256,512]{1,0:T(8,128)}, u32[]{:S(2)}) copy-start(f32[256,512]{1,0:T(8,128)} %copy-done.2) | copy-start | bytes 1572868

commit v2 on v1

--- a/solution.py
+++ b/solution.py
@@ -108,8 +108,16 @@
     spread, held = lax.optimization_barrier((spread, held))
     row_0, row_1 = held[0], held[1]
 
-    lead_rows = lead_rows_from(held)
-    m00, m10, m11 = lead_rows[0, 0], lead_rows[1, 0], lead_rows[1, 1]
+    half = block_size // 2
+    size = block_size * block_size
+    from_row_0 = jnp.concatenate([held[0].ravel(), held[1][:, :half].ravel()])
+    from_row_1 = jnp.concatenate([held[1].ravel(), held[0][half:, :].ravel()])
+    lead_rows = lead_rows_from(jnp.where(row_id == 0, from_row_0, from_row_1))
+    m00 = lead_rows[0, :size].reshape(block_size, block_size)
+    m11 = lead_rows[1, :size].reshape(block_size, block_size)
+    m10 = jnp.concatenate(
+        [lead_rows[0, size:].reshape(block_size, half).T, lead_rows[1, size:].reshape(half, block_size)]
+    )
     spread, m00 = lax.optimization_barrier((spread, m00))
 
     send = jnp.broadcast_to(spread[None], (row_devs,) + spread.shape)

time: 235 us -> 223 us (0.949)
  waiting for transfers between devices: 50.9 us -> 46.1 us
  local copies, waits for them, and re-layouts: 20.4 us -> 17.5 us
  blocking collectives: 24.5 us -> 21.7 us
    all_to_all x1, waiting for transfers between devices: 24.9 us -> 20 us  [lead_rows_from(): gathered = lax.all_to_all(send, 'row', 0, 0)]
    all_to_all x1, blocking collectives: 24.5 us -> 21.7 us  [lead_rows_from(): piece = lax.all_to_all(send, 'row', 0, 0)[:PANELS]]
where the time goes in v2:
time: 223 us; the launch traced here: 219 us
  other arithmetic  95.6 us (43%)
  waiting for transfers between devices  46.1 us (21%)
  starting transfers between devices  25.7 us (12%)
  blocking collectives  21.7 us (10%)
  local copies, waits for them, and re-layouts  17.5 us (8%)
  matrix products  11.8 us (5%)
    another operation x12, other arithmetic, blocked_factor(): diag = jnp.linalg.cholesky(blocks[k][k])  49.9 us
    another operation x8, other arithmetic, blocked_factor(): inv = solve_triangular(diag, eye, lower=True)  42 us
    ppermute x2, waiting for transfers between devices, tree_round(): got = lax.ppermute(payload, 'col', pairs)  26.1 us
    all_to_all x1, blocking collectives, lead_rows_from(): piece = lax.all_to_all(send, 'row', 0, 0)[:PANELS]  21.7 us
    all_to_all x1, waiting for transfers between devices, lead_rows_from(): gathered = lax.all_to_all(send, 'row', 0, 0)  20 us
    all_to_all x1, starting transfers between devices, shards(): spread = lax.all_to_all(send, 'row', 0, 0)[:PANELS]  11.7 us
    dot_general x8, matrix products, dot(): return jnp.dot(a, b, precision=HIGHEST)  7.56 us
    all_to_all x1, starting transfers between devices, lead_rows_from(): gathered = lax.all_to_all(send, 'row', 0, 0)  5.75 us
  transfers between devices with their start and end apart: 6, of which 2 were waited for; matrix products, arithmetic and copies ran while one was open for 24% of the time, Pallas kernels for 0%

profile of v2, /device:TPU:26, one launch (start us, length us, event | category | flops | bytes accessed | tf_op | source)
XLA Modules:
  0.0 219.2 jit_solution(2158173295394002555)
XLA Ops:
  0.0 1.5 copy.86
  2.3 1.2 copy.76
  3.5 11.7 %all-to-all-start = ((f32[32,8,4,256]{3,2,1,0:T(4,128)}), f32[32,8,4,256]{3,2,1,0:T(4,128)}, u32[]{:S(2)}, u32[]{:S(2)}) async-start(f32[32,8,4,256]{3,2,1,0:T(4,128)} %bitcast.29), calls=%async_computation | async-start | bytes 2097152 | tf_op jit(solution)/shard_map/all_to_all | solution.py:107
  15.3 0.7 collective-permute-start.1
  16.1 1.3 collective-permute-start.2
  17.4 26.1 %collective-permute-done.2 = f32[2,256,256]{2,1,0:T(8,128)S(1)} collective-permute-done((f32[2,256,256]{2,1,0:T(8,128)S(1)}, f32[2,256,256]{2,1,0:T(8,128)S(1)}, u32[]{:S(2)}, u32[]{:S(2)}) %collective-permute-start.2) | collective-permute-done | bytes 524320 | tf_op jit(solution)/shard_map/ppermute | solution.py:26
  43.6 0.8 slice.117
  45.0 21.7 %all_to_all.21 = f32[32,1,3072]{2,1,0:T(1,128)S(1)} all-to-all(f32[32,1,3072]{2,1,0:T(1,128)S(1)} %bitcast.112), channel_id=1, replica_groups=mesh['row'=32,'col'=8] {'row'}, dimensions={0} | all-to-all | bytes 786432 | tf_op jit(solution)/shard_map/all_to_all | solution.py:88
  66.7 1.1 broadcast_in_dim.23
  67.8 5.7 %all-to-all-start.2 = ((f32[32,2,3072]{2,1,0:T(2,128)}), f32[32,2,3072]{2,1,0:T(2,128)S(1)}, u32[]{:S(2)}, u32[]{:S(2)}) async-start(f32[32,2,3072]{2,1,0:T(2,128)} %broadcast_in_dim.23), calls=%async_computation.2 | async-start | bytes 1572864 | tf_op jit(solution)/shard_map/all_to_all | solution.py:90
  73.5 20.0 %all-to-all-done.2 = f32[32,2,3072]{2,1,0:T(2,128)S(1)} async-done(((f32[32,2,3072]{2,1,0:T(2,128)}), f32[32,2,3072]{2,1,0:T(2,128)S(1)}, u32[]{:S(2)}, u32[]{:S(2)}) %all-to-all-start.2) | async-done | bytes 786464 | tf_op jit(solution)/shard_map/all_to_all | solution.py:90
  94.0 1.4 slice_reduce_fusion.1
  95.7 11.7 %cholesky.74 = f32[128,128]{1,0:T(8,128)S(1)} custom-call(f32[128,128]{1,0:T(8,128)S(1)} %fusion.37), custom_call_target="Cholesky" | custom-call | tf_op jit(solution)/shard_map/jit(cholesky)/cholesky | solution.py:49
  108.7 9.8 %custom-call.8 = f32[1,128,128]{1,2,0:T(8,128)S(1)} custom-call(f32[1,128,128]{2,1,0:T(8,128)S(1)} %get-tuple-element.35), custom_call_target="InvertDiagBlocksLowerTriangular" | custom-call | tf_op jit(solution)/shard_map/jit(_solve_triangular)/triangular_solve | solution.py:50
  120.1 12.1 %cholesky.85 = f32[128,128]{1,0:T(8,128)S(1)} custom-call(f32[128,128]{1,0:T(8,128)S(1)} %fusion.35), custom_call_target="Cholesky" | custom-call | tf_op jit(solution)/shard_map/jit(cholesky)/cholesky | solution.py:49
  133.5 9.8 %custom-call.9 = f32[1,128,128]{1,2,0:T(8,128)S(1)} custom-call(f32[1,128,128]{2,1,0:T(8,128)S(1)} %get-tuple-element.33), custom_call_target="InvertDiagBlocksLowerTriangular" | custom-call | tf_op jit(solution)/shard_map/jit(_solve_triangular)/triangular_solve | solution.py:50
  143.6 1.8 broadcast_in_dim.24
  145.4 5.6 %all-to-all-start.3 = ((f32[32,2,8,4,256]{4,3,2,1,0:T(4,128)}), f32[32,2,8,4,256]{4,3,2,1,0:T(4,128)}, u32[]{:S(2)}, u32[]{:S(2)}) async-start(f32[32,2,8,4,256]{4,3,2,1,0:T(4,128)} %broadcast_in_dim.24), calls=%async_computation.3 | async-start | bytes 4194304 | tf_op jit(solution)/shard_map/all_to_all | solution.py:124
  152.9 11.7 %cholesky.96 = f32[128,128]{1,0:T(8,128)S(1)} custom-call(f32[128,128]{1,0:T(8,128)S(1)} %fusion.33), custom_call_target="Cholesky" | custom-call | tf_op jit(solution)/shard_map/jit(cholesky)/cholesky | solution.py:49
  165.9 9.8 %custom-call.10 = f32[1,128,128]{1,2,0:T(8,128)S(1)} custom-call(f32[1,128,128]{2,1,0:T(8,128)S(1)} %get-tuple-element.31), custom_call_target="InvertDiagBlocksLowerTriangular" | custom-call | tf_op jit(solution)/shard_map/jit(_solve_triangular)/triangular_solve | solution.py:50
  176.8 11.7 %cholesky.107 = f32[128,128]{1,0:T(8,128)S(1)} custom-call(f32[128,128]{1,0:T(8,128)S(1)} %fusion.31), custom_call_target="Cholesky" | custom-call | tf_op jit(solution)/shard_map/jit(cholesky)/cholesky | solution.py:49
  189.8 9.9 %custom-call.11 = f32[1,128,128]{1,2,0:T(8,128)S(1)} custom-call(f32[1,128,128]{2,1,0:T(8,128)S(1)} %get-tuple-element.29), custom_call_target="InvertDiagBlocksLowerTriangular" | custom-call | tf_op jit(solution)/shard_map/jit(_solve_triangular)/triangular_solve | solution.py:50
  201.8 1.0 fusion
  202.8 2.1 copy.65
  205.5 3.6 %fusion.6 = f32[512,1024]{1,0:T(8,128)S(1)} fusion(f32[512,1024]{1,0:T(8,128)S(1)} %bitcast.104, f32[256,256]{1,0:T(8,128)S(1)} %get-tuple-element.45, f32[128,128]{1,0:T(8,128)S(1)} %copy.63, f32[128,128]{1,0:T(8,128)S(1)} %convolution_negate_fusion.1, f32[128,256]{1,0:T(8,128)S(1)} %concatenate.88, f32[256,256]{1,0:T(8,128)S(1)} %convolution_negate_fusion), kind=kOutput, calls=%fused_computation.21 | convolution fusion | flops 3222798336 | bytes 4980736 | tf_op jit(solution)/shard_map/dot_general | solution.py:12
  209.0 1.9 fusion.52
  210.9 1.3 copy.67
  212.2 1.2 reshape.100
  213.5 1.0 slice.133
  214.7 2.3 %broadcast_select_fusion = f32[1,1,256,4,1,256]{5,4,3,2,1,0:T(1,128)} fusion(pred[]{:T(512)S(6)} %ge.12, f32[1,1,256,4,1,256]{5,4,3,2,1,0:T(1,128)S(1)} %copy-done, f32[1,1,256,4,1,256]{5,4,3,2,1,0:T(1,128)S(1)} %reshape.100), kind=kLoop, calls=%fused_computation | loop fusion | flops 524288 | bytes 3145729 | tf_op jit(solution)/shard_map/jit(_where)/select_n | solution.py:146
  217.0 1.0 fusion.8
  218.0 1.0 copy_dynamic-update-slice_fusion
  (81 shorter events, 14.6 us)
Async XLA Ops:
  0.0 2.2 %copy-start = (f32[1,1,256,4,1,256]{5,4,3,2,1,0:T(1,128)S(1)}, f32[1,1,256,4,1,256]{5,4,3,2,1,0:T(1,128)}, u32[]{:S(2)}) copy-start(f32[1,1,256,4,1,256]{5,4,3,2,1,0:T(1,128)} %param.6) | copy-start | bytes 3145732
  1.5 13.7 %copy-start.1 = (f32[1,1,256,4,1,256]{5,2,3,4,1,0:T(8,128)}, f32[1,1,256,4,1,256]{5,2,3,4,1,0:T(8,128)S(1)}, u32[]{:S(2)}) copy-start(f32[1,1,256,4,1,256]{5,2,3,4,1,0:T(8,128)S(1)} %copy.86) | copy-start | bytes 3145732
  1.6 13.6 %collective-permute-start = (f32[256,256]{1,0:T(8,128)S(1)}, f32[256,256]{1,0:T(8,128)S(1)}, u32[]{:S(2)}, u32[]{:S(2)}) collective-permute-start(f32[256,256]{1,0:T(8,128)S(1)} %slice_bitcast_fusion), channel_id=1, source_target_pairs={{0,1},{1,0},{8,9},{9,8},{16,17},{17,16},{24,25},{25,24},{32,33},{3... | collective-permute-start | bytes 786440 | tf_op jit(solution)/shard_map/ppermute | solution.py:38
  3.5 40.1 %all-to-all-start = ((f32[32,8,4,256]{3,2,1,0:T(4,128)}), f32[32,8,4,256]{3,2,1,0:T(4,128)}, u32[]{:S(2)}, u32[]{:S(2)}) async-start(f32[32,8,4,256]{3,2,1,0:T(4,128)} %bitcast.29), calls=%async_computation | async-start | bytes 2097152 | tf_op jit(solution)/shard_map/all_to_all | solution.py:107
  15.3 0.7 collective-permute-start.1
  16.1 27.4 %collective-permute-start.2 = (f32[2,256,256]{2,1,0:T(8,128)S(1)}, f32[2,256,256]{2,1,0:T(8,128)S(1)}, u32[]{:S(2)}, u32[]{:S(2)}) collective-permute-start(f32[2,256,256]{2,1,0:T(8,128)S(1)} %broadcast_select_fusion.1), channel_id=1, source_target_pairs={{0,4},{1,5},{2,6},{3,7},{8,12},{9,13},{10,14},{11,15},{16,20},{17,... | collective-permute-start | bytes 1572872 | tf_op jit(solution)/shard_map/ppermute | solution.py:26
  67.8 25.8 %all-to-all-start.2 = ((f32[32,2,3072]{2,1,0:T(2,128)}), f32[32,2,3072]{2,1,0:T(2,128)S(1)}, u32[]{:S(2)}, u32[]{:S(2)}) async-start(f32[32,2,3072]{2,1,0:T(2,128)} %broadcast_in_dim.23), calls=%async_computation.2 | async-start | bytes 1572864 | tf_op jit(solution)/shard_map/all_to_all | solution.py:90
  145.4 57.4 %all-to-all-start.3 = ((f32[32,2,8,4,256]{4,3,2,1,0:T(4,128)}), f32[32,2,8,4,256]{4,3,2,1,0:T(4,128)}, u32[]{:S(2)}, u32[]{:S(2)}) async-start(f32[32,2,8,4,256]{4,3,2,1,0:T(4,128)} %broadcast_in_dim.24), calls=%async_computation.3 | async-start | bytes 4194304 | tf_op jit(solution)/shard_map/all_to_all | solution.py:124
  202.8 6.2 %copy-start.2 = (f32[256,512]{1,0:T(8,128)}, f32[256,512]{1,0:T(8,128)S(1)}, u32[]{:S(2)}) copy-start(f32[256,512]{1,0:T(8,128)S(1)} %fusion) | copy-start | bytes 1572868
  213.5 3.5 %copy-start.3 = (f32[256,512]{1,0:T(8,128)S(1)}, f32[256,512]{1,0:T(8,128)}, u32[]{:S(2)}) copy-start(f32[256,512]{1,0:T(8,128)} %copy-done.2) | copy-start | bytes 1572868

commit v3 on v2

--- a/solution.py
+++ b/solution.py
@@ -46,7 +46,7 @@
     low = [[None] * count for _ in range(count)]
     inv_diag = []
     for k in range(count):
-        diag = jnp.linalg.cholesky(blocks[k][k])
+        diag = lax.linalg.cholesky(blocks[k][k], symmetrize_input=False)
         inv = solve_triangular(diag, eye, lower=True)
         low[k][k] = diag
         inv_diag.append(inv)
@@ -143,10 +143,13 @@
         jnp.where(row_id == 1, factor[block_size:], left),
     )
     update = dot(left, right).reshape(block_size, cols_local, block_size)
-    trailing = jnp.where(row_id >= PANELS, tiles - update, 0.0)
     panel = jnp.where(col_id == 0, left[:, :block_size], left[:, block_size:])
-    first_col = jnp.where(col_id < PANELS, panel, trailing[:, 0, :])
-    out = trailing.at[:, 0, :].set(first_col)
+    first_local = (jnp.arange(cols_local) == 0)[None, :, None]
+    out = jnp.where(
+        first_local & (col_id < PANELS),
+        panel[:, None, :],
+        jnp.where(row_id >= PANELS, tiles - update, 0.0),
+    )
     return out.reshape(kernel.shape)
 
 

time: 223 us -> 247 us (1.11)
  other arithmetic: 95.6 us -> 106 us
  matrix products: 11.8 us -> 20.1 us
  local copies, waits for them, and re-layouts: 17.5 us -> 23 us
    another operation x8, other arithmetic: 42 us -> 47.7 us  [blocked_factor(): inv = solve_triangular(diag, eye, lower=True)]
    unnamed x17 -> x50, local copies, waits for them, and re-layouts: 3.74 us -> 7.22 us
    another operation x12, other arithmetic: 49.9 us -> 53.2 us  [blocked_factor(): diag = lax.linalg.cholesky(blocks[k][k], symmetrize_input=False)]
    dot_general x8, matrix products: 7.56 us -> 10.2 us  [dot(): return jnp.dot(a, b, precision=HIGHEST)]
  transfers between devices with their start and end apart: 6 -> 6, of which waited for: 2 -> 2; matrix products, arithmetic and copies ran while one was open for 24% -> 31% of each run, Pallas kernels for 0% -> 0%
where the time goes in v3:
time: 247 us; the launch traced here: 243 us
  other arithmetic  106 us (43%)
  waiting for transfers between devices  46.1 us (19%)
  starting transfers between devices  25.6 us (10%)
  local copies, waits for them, and re-layouts  23 us (9%)
  blocking collectives  21.7 us (9%)
  matrix products  20.1 us (8%)
    another operation x12, other arithmetic, blocked_factor(): diag = lax.linalg.cholesky(blocks[k][k], symmetrize_input=False)  53.2 us
    another operation x8, other arithmetic, blocked_factor(): inv = solve_triangular(diag, eye, lower=True)  47.7 us
    ppermute x2, waiting for transfers between devices, tree_round(): got = lax.ppermute(payload, 'col', pairs)  26.1 us
    all_to_all x1, blocking collectives, lead_rows_from(): piece = lax.all_to_all(send, 'row', 0, 0)[:PANELS]  21.7 us
    all_to_all x1, waiting for transfers between devices, lead_rows_from(): gathered = lax.all_to_all(send, 'row', 0, 0)  20 us
    all_to_all x1, starting transfers between devices, shards(): spread = lax.all_to_all(send, 'row', 0, 0)[:PANELS]  11.7 us
    dot_general x8, matrix products, dot(): return jnp.dot(a, b, precision=HIGHEST)  10.2 us
    unnamed x50, local copies, waits for them, and re-layouts  7.22 us
  transfers between devices with their start and end apart: 6, of which 2 were waited for; matrix products, arithmetic and copies ran while one was open for 31% of the time, Pallas kernels for 0%

profile of v3, /device:TPU:26, one launch (start us, length us, event | category | flops | bytes accessed | tf_op | source)
XLA Modules:
  0.0 243.1 jit_solution(16873724949358287821)
XLA Ops:
  0.0 1.5 copy.47
  2.2 1.2 copy.39
  3.5 11.7 %all-to-all-start = ((f32[32,8,4,256]{3,2,1,0:T(4,128)}), f32[32,8,4,256]{3,2,1,0:T(4,128)}, u32[]{:S(2)}, u32[]{:S(2)}) async-start(f32[32,8,4,256]{3,2,1,0:T(4,128)} %bitcast.22), calls=%async_computation | async-start | bytes 2097152 | tf_op jit(solution)/shard_map/all_to_all | solution.py:107
  16.1 1.3 collective-permute-start.2
  17.4 26.1 %collective-permute-done.2 = f32[2,256,256]{2,1,0:T(8,128)S(1)} collective-permute-done((f32[2,256,256]{2,1,0:T(8,128)S(1)}, f32[2,256,256]{2,1,0:T(8,128)S(1)}, u32[]{:S(2)}, u32[]{:S(2)}) %collective-permute-start.2) | collective-permute-done | bytes 524320 | tf_op jit(solution)/shard_map/ppermute | solution.py:26
  45.9 21.7 %all_to_all.21 = f32[32,1,3072]{2,1,0:T(1,128)S(1)} all-to-all(f32[32,1,3072]{2,1,0:T(1,128)S(1)} %bitcast.90), channel_id=1, replica_groups=mesh['row'=32,'col'=8] {'row'}, dimensions={0} | all-to-all | bytes 786432 | tf_op jit(solution)/shard_map/all_to_all | solution.py:88
  68.7 5.8 %all-to-all-start.2 = ((f32[32,2,3072]{2,1,0:T(2,128)}), f32[32,2,3072]{2,1,0:T(2,128)S(1)}, u32[]{:S(2)}, u32[]{:S(2)}) async-start(f32[32,2,3072]{2,1,0:T(2,128)} %broadcast_in_dim.39), calls=%async_computation.2 | async-start | bytes 1572864 | tf_op jit(solution)/shard_map/all_to_all | solution.py:90
  74.5 20.0 %all-to-all-done.2 = f32[32,2,3072]{2,1,0:T(2,128)S(1)} async-done(((f32[32,2,3072]{2,1,0:T(2,128)}), f32[32,2,3072]{2,1,0:T(2,128)S(1)}, u32[]{:S(2)}, u32[]{:S(2)}) %all-to-all-start.2) | async-done | bytes 786464 | tf_op jit(solution)/shard_map/all_to_all | solution.py:90
  94.5 1.4 slice_reduce_fusion.1
  96.4 11.7 %custom-call.12 = f32[128,128]{1,0:T(8,128)S(1)} custom-call(f32[128,128]{1,0:T(8,128)S(1)} %slice.80), custom_call_target="Cholesky" | custom-call | tf_op jit(solution)/shard_map/cholesky/custom-call.1 | solution.py:49
  108.8 1.3 select_bitcast_fusion.5
  110.1 9.8 %custom-call.13 = f32[1,128,128]{1,2,0:T(8,128)S(1)} custom-call(f32[1,128,128]{2,1,0:T(8,128)S(1)} %get-tuple-element.23), custom_call_target="InvertDiagBlocksLowerTriangular" | custom-call | tf_op jit(solution)/shard_map/jit(_solve_triangular)/triangular_solve | solution.py:50
  123.7 12.1 %custom-call.14 = f32[128,128]{1,0:T(8,128)S(1)} custom-call(f32[128,128]{1,0:T(8,128)S(1)} %convolution_subtract_fusion.2), custom_call_target="Cholesky" | custom-call | tf_op jit(solution)/shard_map/cholesky/custom-call.1 | solution.py:49
  136.5 1.3 select_bitcast_fusion.4
  137.9 9.8 %custom-call.15 = f32[1,128,128]{1,2,0:T(8,128)S(1)} custom-call(f32[1,128,128]{2,1,0:T(8,128)S(1)} %get-tuple-element.21), custom_call_target="InvertDiagBlocksLowerTriangular" | custom-call | tf_op jit(solution)/shard_map/jit(_solve_triangular)/triangular_solve | solution.py:50
  148.1 1.9 broadcast_in_dim.41
  149.9 5.6 %all-to-all-start.3 = ((f32[32,2,8,4,256]{4,3,2,1,0:T(4,128)}), f32[32,2,8,4,256]{4,3,2,1,0:T(4,128)S(1)}, u32[]{:S(2)}, u32[]{:S(2)}) async-start(f32[32,2,8,4,256]{4,3,2,1,0:T(4,128)} %broadcast_in_dim.41), calls=%async_computation.3 | async-start | bytes 4194304 | tf_op jit(solution)/shard_map/all_to_all | solution.py:124
  156.7 1.4 fusion.9
  158.9 1.5 convolution_subtract_fusion
  161.8 12.5 %custom-call.16 = f32[128,128]{1,0:T(8,128)S(1)} custom-call(f32[128,128]{1,0:T(8,128)} %slice.99), custom_call_target="Cholesky" | custom-call | tf_op jit(solution)/shard_map/cholesky/custom-call.1 | solution.py:49
  176.3 10.6 %custom-call.17 = f32[1,128,128]{1,2,0:T(8,128)S(1)} custom-call(f32[1,128,128]{2,1,0:T(8,128)} %get-tuple-element.19), custom_call_target="InvertDiagBlocksLowerTriangular" | custom-call | tf_op jit(solution)/shard_map/jit(_solve_triangular)/triangular_solve | solution.py:50
  189.7 1.8 convolution_subtract_fusion.1
  191.4 13.2 %custom-call.18 = f32[128,128]{1,0:T(8,128)} custom-call(f32[128,128]{1,0:T(8,128)} %convolution_subtract_fusion.1), custom_call_target="Cholesky" | custom-call | tf_op jit(solution)/shard_map/cholesky/custom-call.1 | solution.py:49
  206.2 2.2 select_bitcast_fusion.2
  208.4 11.4 %custom-call.19 = f32[1,128,128]{1,2,0:T(8,128)} custom-call(f32[1,128,128]{2,1,0:T(8,128)} %get-tuple-element.17), custom_call_target="InvertDiagBlocksLowerTriangular" | custom-call | tf_op jit(solution)/shard_map/jit(_solve_triangular)/triangular_solve | solution.py:50
  219.8 1.7 fusion.18
  221.5 1.6 copy.32
  227.5 1.5 fusion.42
  233.4 3.5 %fusion.6 = f32[512,1024]{1,0:T(8,128)S(1)} fusion(f32[512,1024]{1,0:T(8,128)S(1)} %bitcast.84, f32[256,256]{1,0:T(8,128)S(1)} %copy-done.6, f32[128,128]{1,0:T(8,128)S(1)} %copy-done.11, f32[128,128]{1,0:T(8,128)S(1)} %convolution_negate_fusion.1, f32[128,256]{1,0:T(8,128)S(1)} %copy-done.4, f32[256,256]{1,0:T(8,128)S(1)} %convolution_negate_fusion), kind=kOutput, calls=%fused_computation.22 | convolution fusion | flops 3222798336 | bytes 4980736 | tf_op jit(solution)/shard_map/dot_general | solution.py:12
  237.0 1.9 fusion.46
  238.9 1.2 reshape.66
  240.2 2.8 %broadcast_select_fusion = f32[1,1,256,4,1,256]{5,4,3,2,1,0:T(1,128)} fusion(pred[4]{0:T(512)(128)(4,1)S(1)} %compare_and_fusion, pred[]{:T(512)S(6)} %ge.24, f32[1,1,256,4,1,256]{5,4,3,2,1,0:T(1,128)S(1)} %copy-done, f32[1,1,256,4,1,256]{5,4,3,2,1,0:T(1,128)S(1)} %reshape.66, f32[256,256]{1,0:T(8,128)S(1)} %copy-done.8), kind=kLoop, calls=%fused_computation | loop fusion | flops 786432 | bytes 3407877 | tf_op jit(solution)/shard_map/jit(_where)/select_n | solution.py:148
  (102 shorter events, 29.4 us)
Async XLA Ops:
  0.0 2.2 copy-start
  1.5 13.6 %collective-permute-start = (f32[256,256]{1,0:T(8,128)S(1)}, f32[256,256]{1,0:T(8,128)S(1)}, u32[]{:S(2)}, u32[]{:S(2)}) collective-permute-start(f32[256,256]{1,0:T(8,128)S(1)} %slice_bitcast_fusion), channel_id=1, source_target_pairs={{0,1},{1,0},{8,9},{9,8},{16,17},{17,16},{24,25},{25,24},{32,33},{3... | collective-permute-start | bytes 786440 | tf_op jit(solution)/shard_map/ppermute | solution.py:38
  3.5 40.1 %all-to-all-start = ((f32[32,8,4,256]{3,2,1,0:T(4,128)}), f32[32,8,4,256]{3,2,1,0:T(4,128)}, u32[]{:S(2)}, u32[]{:S(2)}) async-start(f32[32,8,4,256]{3,2,1,0:T(4,128)} %bitcast.22), calls=%async_computation | async-start | bytes 2097152 | tf_op jit(solution)/shard_map/all_to_all | solution.py:107
  15.3 0.7 collective-permute-start.1
  16.1 27.4 %collective-permute-start.2 = (f32[2,256,256]{2,1,0:T(8,128)S(1)}, f32[2,256,256]{2,1,0:T(8,128)S(1)}, u32[]{:S(2)}, u32[]{:S(2)}) collective-permute-start(f32[2,256,256]{2,1,0:T(8,128)S(1)} %broadcast_select_fusion.2), channel_id=1, source_target_pairs={{0,4},{1,5},{2,6},{3,7},{8,12},{9,13},{10,14},{11,15},{16,20},{17,... | collective-permute-start | bytes 1572872 | tf_op jit(solution)/shard_map/ppermute | solution.py:26
  45.2 0.7 copy-start.14
  68.7 25.8 %all-to-all-start.2 = ((f32[32,2,3072]{2,1,0:T(2,128)}), f32[32,2,3072]{2,1,0:T(2,128)S(1)}, u32[]{:S(2)}, u32[]{:S(2)}) async-start(f32[32,2,3072]{2,1,0:T(2,128)} %broadcast_in_dim.39), calls=%async_computation.2 | async-start | bytes 1572864 | tf_op jit(solution)/shard_map/all_to_all | solution.py:90
  148.0 8.0 %copy-start.13 = (f32[128,128]{1,0:T(8,128)}, f32[128,128]{1,0:T(8,128)S(1)}, u32[]{:S(2)}) copy-start(f32[128,128]{1,0:T(8,128)S(1)} %copy.28) | copy-start | bytes 196612
  149.9 82.1 %all-to-all-start.3 = ((f32[32,2,8,4,256]{4,3,2,1,0:T(4,128)}), f32[32,2,8,4,256]{4,3,2,1,0:T(4,128)S(1)}, u32[]{:S(2)}, u32[]{:S(2)}) async-start(f32[32,2,8,4,256]{4,3,2,1,0:T(4,128)} %broadcast_in_dim.41), calls=%async_computation.3 | async-start | bytes 4194304 | tf_op jit(solution)/shard_map/all_to_all | solution.py:124
  156.1 0.6 copy-start.12
  160.5 0.7 copy-start.9
  187.2 0.6 copy-start.7
  223.1 5.9 %copy-start.10 = (f32[128,128]{1,0:T(8,128)S(1)}, f32[128,128]{1,0:T(8,128)}, u32[]{:S(2)}) copy-start(f32[128,128]{1,0:T(8,128)} %copy.32) | copy-start | bytes 196612
  223.1 6.3 %copy-start.15 = (f32[256,256]{1,0:T(8,128)S(1)}, f32[256,256]{1,0:T(8,128)}, u32[]{:S(2)}) copy-start(f32[256,256]{1,0:T(8,128)} %copy-done.14) | copy-start | bytes 786436
  223.1 6.3 %copy-start.16 = (f32[256,256]{1,0:T(8,128)S(1)}, f32[256,256]{1,0:T(8,128)}, u32[]{:S(2)}) copy-start(f32[256,256]{1,0:T(8,128)} %copy.30) | copy-start | bytes 786436
  223.1 6.3 %copy-start.17 = (f32[256,256]{1,0:T(8,128)S(1)}, f32[256,256]{1,0:T(8,128)}, u32[]{:S(2)}) copy-start(f32[256,256]{1,0:T(8,128)} %get-tuple-element.29) | copy-start | bytes 786436
  223.1 6.3 %copy-start.18 = (f32[128,128]{1,0:T(8,128)S(1)}, f32[128,128]{1,0:T(8,128)}, u32[]{:S(2)}) copy-start(f32[128,128]{1,0:T(8,128)} %get-tuple-element.20) | copy-start | bytes 196612
  223.1 6.3 %copy-start.19 = (f32[128,128]{1,0:T(8,128)S(1)}, f32[128,128]{1,0:T(8,128)}, u32[]{:S(2)}) copy-start(f32[128,128]{1,0:T(8,128)} %get-tuple-element.18) | copy-start | bytes 196612
  223.1 6.3 %copy-start.20 = (f32[128,128]{1,0:T(8,128)S(1)}, f32[128,128]{1,0:T(8,128)}, u32[]{:S(2)}) copy-start(f32[128,128]{1,0:T(8,128)} %copy.29) | copy-start | bytes 196612
  224.1 6.4 %copy-start.3 = (f32[128,256]{1,0:T(8,128)}, f32[128,256]{1,0:T(8,128)S(1)}, u32[]{:S(2)}) copy-start(f32[128,256]{1,0:T(8,128)S(1)} %concatenate.86) | copy-start | bytes 393220
  225.1 5.3 %copy-start.5 = (f32[256,256]{1,0:T(8,128)}, f32[256,256]{1,0:T(8,128)S(1)}, u32[]{:S(2)}) copy-start(f32[256,256]{1,0:T(8,128)S(1)} %get-tuple-element.33) | copy-start | bytes 786436
  230.5 0.8 copy-start.1
  232.4 0.9 copy-start.4
  232.4 1.0 copy-start.6
  232.4 1.0 copy-start.11
  233.4 3.6 %copy-start.2 = (f32[256,512]{1,0:T(8,128)S(1)}, f32[256,512]{1,0:T(8,128)}, u32[]{:S(2)}) copy-start(f32[256,512]{1,0:T(8,128)} %copy-done.1) | copy-start | bytes 1572868
  237.0 3.2 %copy-start.8 = (f32[256,256]{1,0:T(8,128)S(1)}, f32[256,256]{1,0:T(8,128)}, u32[]{:S(2)}) copy-start(f32[256,256]{1,0:T(8,128)} %slice_select_fusion) | copy-start | bytes 786436
